TPU v7x, 512 devices: a whole 4x4x16 slice. The times are simulated.
512 devices in a mesh: inst: 16 (over y_lo, x, core), blk: 32 (over z, y_hi).
Axes of the slice: x: 4, y: 4 (y_hi: 2, y_lo: 2; y = y_hi * 2 + y_lo), z: 16, core: 2. Of those that a mesh axis runs over, the one named last changes fastest.
Arguments:
- state: float32 [16, 2, 6, 8, 8, 4096], P('inst', None, None, None, None, 'blk'), may hold values from -0.5 to 3, as said below
- donor_block: int32 [16, 2, 32], P('inst', None, 'blk'), may hold values from 0 to 31, as said below
- donor_offset: int32 [16, 2, 32], P('inst', None, 'blk'), may hold values from 0 to 127, as said below
Outputs:
- hb_residual: float32 [16, 2, 6, 8, 8, 4096], P('inst', None, None, None, None, 'blk')
- new_state: float32 [16, 2, 6, 8, 8, 4096], P('inst', None, None, None, None, 'blk')
Inputs may be any that keep to these rules, and one draw needn't show every extreme that they name: For each instance n and row r there is one rotation R with donor_block[n, r, b] = (b + R) mod 32 for every block b. `donor_offset`: for each instance and row the offset is the same for all blocks. `state`: density lies in [0.8, 1.25], momenta in [-0.5, 0.5], total energy in [2, 3], turbulence variable in [0.05, 0.5].
All inputs are finite; a program needn't handle non-finite values.
Results may differ from a plain program's by a relative error of at most 0.0003.
Values sent between devices are 32-bit elements; how exact they have to be, the bound alone decides.
No kernel may reach another device: no remote copies, remote signals or barrier semaphores. Data moves between devices by JAX's collectives and lax.ppermute only.
A program may use at most 64 MiB of HBM per device.

v0:
```python
import jax
import jax.numpy as jnp
from jax import lax
from jax.sharding import PartitionSpec as P

gamma_ratio = 1.4
second_coef = 0.5
fourth_coef = 1.0 / 32.0
courant = 0.8
frequency = 0.5
highest = lax.Precision.HIGHEST


def padded_2(block, sides, width):
    for axis, dim in sides:
        count = lax.axis_size(axis)
        forward = [(i, i + 1) for i in range(count - 1)]
        forward.append((count - 1, 0))
        backward = [(target, source) for source, target in forward]
        low = lax.ppermute(
            lax.slice_in_dim(block, block.shape[dim] - width, None, axis=dim), axis, forward
        )
        high = lax.ppermute(lax.slice_in_dim(block, 0, width, axis=dim), axis, backward)
        block = jnp.concatenate([low, block, high], axis=dim)
    return block


def spectral_weights(target, source, number):
    distance = jnp.mod(target - source, number)
    angle = jnp.pi / number * distance.astype(jnp.float32)
    parity = 1.0 - 2.0 * jnp.mod(distance, 2).astype(jnp.float32)
    nonzero = distance != 0
    sine_safe = jnp.where(nonzero, jnp.sin(angle), 1.0)
    cotangent = jnp.where(nonzero, jnp.cos(angle) / sine_safe, 0.0)
    return parity * (0.25 * frequency + 0.5 * frequency * cotangent)


def take_range(array, begin, length, along):
    return lax.slice_in_dim(array, begin, begin + length, axis=along)


def flux_divergence(extended, along):
    length = extended.shape[along] - 4
    cell_axis = along - 1
    density = extended[0]
    inverse = 1.0 / density
    normal_vel = extended[along] * inverse
    kinetic = 0.5 * (extended[1] ** 2 + extended[2] ** 2 + extended[3] ** 2) * inverse
    pressure = (gamma_ratio - 1.0) * (extended[4] - kinetic)
    sound = jnp.sqrt(gamma_ratio * pressure * inverse)
    momentum_flux = []
    for component in (1, 2, 3):
        if component == along:
            momentum_flux.append(extended[component] * normal_vel + pressure)
        else:
            momentum_flux.append(extended[component] * normal_vel)
    fluxes = jnp.stack(
        [extended[along]]
        + momentum_flux
        + [(extended[4] + pressure) * normal_vel, extended[5] * normal_vel]
    )
    radius = jnp.abs(normal_vel) + sound
    p_plus = take_range(pressure, 2, length + 2, cell_axis)
    p_here = take_range(pressure, 1, length + 2, cell_axis)
    p_minus = take_range(pressure, 0, length + 2, cell_axis)
    sensor = jnp.abs(p_plus - 2.0 * p_here + p_minus) / (p_plus + 2.0 * p_here + p_minus)
    spread = 0.5 * (
        take_range(radius, 1, length + 1, cell_axis) + take_range(radius, 2, length + 1, cell_axis)
    )
    eps_two = second_coef * jnp.maximum(
        take_range(sensor, 0, length + 1, cell_axis), take_range(sensor, 1, length + 1, cell_axis)
    )
    eps_four = jnp.maximum(0.0, fourth_coef - eps_two)
    first_diff = take_range(extended, 2, length + 1, along) - take_range(
        extended, 1, length + 1, along
    )
    third_diff = (
        take_range(extended, 3, length + 1, along)
        - 3.0 * take_range(extended, 2, length + 1, along)
        + 3.0 * take_range(extended, 1, length + 1, along)
        - take_range(extended, 0, length + 1, along)
    )
    interface = 0.5 * (
        take_range(fluxes, 1, length + 1, along) + take_range(fluxes, 2, length + 1, along)
    ) - spread * (eps_two * first_diff - eps_four * third_diff)
    return take_range(interface, 1, length, along) - take_range(interface, 0, length, along)


def wall_extend(block):
    mirror_sign = jnp.array([1.0, 1.0, -1.0, 1.0, 1.0, 1.0], jnp.float32).reshape(6, 1, 1, 1)
    lower_ghost = block[:, :, 0:2][:, :, ::-1] * mirror_sign
    upper_ghost = block[:, :, -2:][:, :, ::-1] * mirror_sign
    return jnp.concatenate([lower_ghost, block, upper_ghost], axis=2)


def row_residual(block, low_ghost, high_ghost, circum_ext):
    axial_ext = jnp.concatenate([low_ghost, block, high_ghost], axis=1)
    return (
        flux_divergence(axial_ext, 1)
        + flux_divergence(wall_extend(block), 2)
        + flux_divergence(circum_ext, 3)
    )


def local_step(fields, number):
    inverse = 1.0 / fields[:, 0]
    kinetic = 0.5 * (fields[:, 1] ** 2 + fields[:, 2] ** 2 + fields[:, 3] ** 2) * inverse
    pressure = (gamma_ratio - 1.0) * (fields[:, 4] - kinetic)
    sound = jnp.sqrt(gamma_ratio * pressure * inverse)
    speeds = (jnp.abs(fields[:, 1]) + jnp.abs(fields[:, 2]) + jnp.abs(fields[:, 3])) * inverse
    return courant / (speeds + 3.0 * sound + frequency * number / 2.0)


def donor_faces(all_faces, donor, shift_cells, total_blocks, width):
    first_face = lax.dynamic_index_in_dim(all_faces, donor, 0, keepdims=False)
    second_face = lax.dynamic_index_in_dim(
        all_faces, jnp.mod(donor + 1, total_blocks), 0, keepdims=False
    )
    joined = jnp.concatenate([first_face, second_face], axis=3)
    return lax.dynamic_slice_in_dim(joined, shift_cells, width, axis=3)


def per_device(state, donor_block, donor_offset):
    number = lax.axis_size("inst")
    total_blocks = lax.axis_size("blk")
    own_instance = lax.axis_index("inst")
    fields = state[0]
    width = fields.shape[-1]
    padded = padded_2(state, (("blk", 5),), 2)[0]
    outlet = state[:, 0, :, -2:]
    inlet = state[:, 1, :, 0:2]
    outlet_all, inlet_all = (
        lax.all_gather(outlet, "blk", axis=0, tiled=True),
        lax.all_gather(inlet, "blk", axis=0, tiled=True),
    )
    rotor_high = donor_faces(
        inlet_all, donor_block[0, 0, 0], donor_offset[0, 0, 0], total_blocks, width
    )
    stator_low = donor_faces(
        outlet_all, donor_block[0, 1, 0], donor_offset[0, 1, 0], total_blocks, width
    )
    piece = lax.all_gather(state, "inst", axis=0, tiled=True)
    sources = jnp.arange(piece.shape[0], dtype=jnp.int32)
    weights = spectral_weights(own_instance, sources, number)
    spectral = jnp.tensordot(weights, piece, axes=(0, 0), precision=highest)
    rotor = fields[0]
    stator = fields[1]
    rotor_low = jnp.concatenate([rotor[:, 0:1], rotor[:, 0:1]], axis=1)
    stator_high = jnp.concatenate([stator[:, -1:], stator[:, -1:]], axis=1)
    rotor_res = row_residual(rotor, rotor_low, rotor_high, padded[0])
    stator_res = row_residual(stator, stator_low, stator_high, padded[1])
    residual = jnp.stack([rotor_res, stator_res]) + spectral
    step = local_step(fields, number)
    updated = fields - step[:, None] * residual
    return (residual[None], updated[None])


def solution(mesh):
    return jax.shard_map(
        per_device,
        mesh=mesh,
        in_specs=(
            P("inst", None, None, None, None, "blk"),
            P("inst", None, "blk"),
            P("inst", None, "blk"),
        ),
        out_specs=(
            P("inst", None, None, None, None, "blk"),
            P("inst", None, None, None, None, "blk"),
        ),
        check_vma=False,
    )
```

profile of v0, /device:TPU:1, one launch (start us, length us, event | category | flops | bytes accessed | tf_op | source)
XLA Modules:
  0.0 371.4 jit_solution(17688199115417346570)
XLA Ops:
  7.2 0.0 copy-start
  7.2 0.0 copy-start.4
  7.2 0.0 all-gather.8.cloned.1.call-start
  7.2 1.5 fusion.181
  8.7 0.0 all-gather.8.cloned.1.call-update
  8.8 0.0 all-gather.10.cloned.1.call-start
  8.8 0.7 all-gather.10.cloned.1.call-update
  9.5 0.0 all-gather.6.cloned.1.call-start
  9.6 0.7 all-gather.6.cloned.1.call-update
  10.3 1.3 fusion.182
  11.5 5.6 %collective-permute-start = (f32[1,2,6,8,8,2]{5,4,3,2,1,0:T(8,128)S(1)}, f32[1,2,6,8,8,2]{5,4,3,2,1,0:T(8,128)S(1)}, u32[]{:S(2)}, u32[]{:S(2)}) collective-permute-start(f32[1,2,6,8,8,2]{5,4,3,2,1,0:T(8,128)S(1)} %get-tuple-element.69), channel_id=1, source_target_pairs={{0,1},{1,2},{2,3},{3,4},{4,5},{5,6},{6,7},{7,8},{8,9},{9,10},{10,1... | collective-permute-start | bytes 18440 | tf_op jit(solution)/shard_map/ppermute | solution.py:20
  17.2 10.9 %collective-permute-start.1 = (f32[1,2,6,8,8,2]{5,4,3,2,1,0:T(8,128)S(1)}, f32[1,2,6,8,8,2]{5,4,3,2,1,0:T(8,128)S(1)}, u32[]{:S(2)}, u32[]{:S(2)}) collective-permute-start(f32[1,2,6,8,8,2]{5,4,3,2,1,0:T(8,128)S(1)} %get-tuple-element.70), channel_id=1, source_target_pairs={{1,0},{2,1},{3,2},{4,3},{5,4},{6,5},{7,6},{8,7},{9,8},{10,9},{11,1... | collective-permute-start | bytes 18440 | tf_op jit(solution)/shard_map/ppermute | solution.py:23
  28.0 1.1 slice_bitcast_fusion.3
  29.1 0.0 copy-start.5
  29.2 0.1 rev.13
  29.3 0.1 rev.12
  29.4 0.1 rev.15
  29.5 0.1 rev.14
  29.7 0.8 broadcast_multiply_fusion.6
  30.5 0.1 pad_maximum_fusion.5
  30.6 0.1 fusion.109
  30.7 0.1 fusion.90
  30.8 0.0 copy-done
  30.8 0.7 fusion.111
  32.0 0.0 copy-done.4
  32.0 0.6 fusion.185
  32.6 0.4 fusion.26
  33.0 0.4 fusion.12
  33.3 0.0 copy-done.5
  33.4 0.6 fusion.186
  40.6 0.6 slice.693
  41.2 0.6 slice.758
  44.4 0.0 collective-permute-done
  44.4 0.0 collective-permute-done.1
  44.4 0.4 pad_maximum_fusion
  44.8 0.1 fusion.96
  44.9 0.1 fusion.69
  45.0 0.1 add_divide_fusion.2
  45.1 0.0 copy-start.2
  45.1 0.0 copy-start.3
  45.2 0.1 fusion.64
  45.3 0.1 add_divide_fusion
  45.4 0.1 subtract_maximum_fusion
  45.5 0.1 subtract_maximum_fusion.2
  45.8 0.1 slice_bitcast_fusion.1
  45.9 1.1 fusion.5
  47.0 107.0 %all-gather.8.cloned.1.call-done = f32[32,1,6,2,8,128]{5,4,3,2,1,0:T(8,128)} async-done(((f32[1,1,6,2,8,128]{5,4,3,2,1,0:T(8,128)}), f32[32,1,6,2,8,128]{5,4,3,2,1,0:T(8,128)}) %all-gather.8.cloned.1.call-update) | async-done | bytes 1572880 | tf_op jit(solution)/shard_map/all_gather | solution.py:134
  153.9 0.8 dynamic-slice_bitcast_fusion.2
  154.8 0.1 fusion.113
  154.9 143.0 %all-gather.10.cloned.1.call-done = f32[32,1,6,2,8,128]{5,4,3,2,1,0:T(8,128)} async-done(((f32[1,1,6,2,8,128]{5,4,3,2,1,0:T(8,128)}), f32[32,1,6,2,8,128]{5,4,3,2,1,0:T(8,128)}) %all-gather.10.cloned.1.call-update) | async-done | bytes 1572880 | tf_op jit(solution)/shard_map/all_gather | solution.py:133
  297.8 0.8 dynamic-slice_bitcast_fusion
  298.7 0.1 fusion.112
  298.8 0.0 copy-done.2
  298.8 0.0 copy-done.3
  299.2 0.0 copy-start.1
  299.3 0.1 fusion.44
  299.5 0.1 fusion.38
  299.6 0.1 fusion.53
  299.7 0.1 fusion.50
  299.8 54.4 %all-gather.6.cloned.1.call-done = f32[16,2,6,8,8,128]{5,4,3,2,1,0:T(8,128)} async-done(((f32[1,2,6,8,8,128]{5,4,3,2,1,0:T(8,128)}), f32[16,2,6,8,8,128]{5,4,3,2,1,0:T(8,128)}) %all-gather.6.cloned.1.call-update) | async-done | bytes 6291472 | tf_op jit(solution)/shard_map/all_gather | solution.py:142
  354.2 9.6 %fusion = f32[1,2,6,8,8,128]{5,0,4,3,2,1:T(1,128)S(1)} fusion(f32[16,2,6,8,8,128]{5,4,3,2,1,0:T(8,128)} %all-gather.6.cloned.1.call-done, s32[]{:T(128)S(6)} %axis_index.15), kind=kOutput, calls=%fused_computation | convolution fusion | flops 18874928 | bytes 6684676 | tf_op jit(solution)/shard_map/dot_general | solution.py:145
  363.9 0.0 copy-done.1
  363.9 1.0 subtract_bitcast_fusion
  (55 shorter events, 1.0 us)
Async XLA Ops:
  7.2 23.6 %copy-start = (f32[1,2,6,8,8,128]{5,4,3,2,1,0:T(8,128)S(1)}, f32[1,2,6,8,8,128]{5,4,3,2,1,0:T(8,128)}, u32[]{:S(2)}) copy-start(f32[1,2,6,8,8,128]{5,4,3,2,1,0:T(8,128)} %param.5) | copy-start | bytes 1179652
  7.2 24.8 %copy-start.4 = (s32[1,2,1]{1,2,0:T(1,128)S(1)}, s32[1,2,1]{1,2,0:T(1,128)}, u32[]{:S(2)}) copy-start(s32[1,2,1]{1,2,0:T(1,128)} %param.6) | copy-start | bytes 28
  7.2 146.7 %all-gather.8.cloned.1.call-start = ((), (), s32[]{:S(2)}) async-start(), calls=%async_computation.1 | async-start | bytes 1622016 | tf_op jit(solution)/shard_map/all_gather | solution.py:134
  8.8 289.1 %all-gather.10.cloned.1.call-start = ((), (), s32[]{:S(2)}) async-start(), calls=%async_computation.2 | async-start | bytes 1622016 | tf_op jit(solution)/shard_map/all_gather | solution.py:133
  9.5 344.7 %all-gather.6.cloned.1.call-start = ((), (), s32[]{:S(2)}) async-start(), calls=%async_computation | async-start | bytes 6684672 | tf_op jit(solution)/shard_map/all_gather | solution.py:142
  11.5 32.8 %collective-permute-start = (f32[1,2,6,8,8,2]{5,4,3,2,1,0:T(8,128)S(1)}, f32[1,2,6,8,8,2]{5,4,3,2,1,0:T(8,128)S(1)}, u32[]{:S(2)}, u32[]{:S(2)}) collective-permute-start(f32[1,2,6,8,8,2]{5,4,3,2,1,0:T(8,128)S(1)} %get-tuple-element.69), channel_id=1, source_target_pairs={{0,1},{1,2},{2,3},{3,4},{4,5},{5,6},{6,7},{7,8},{8,9},{9,10},{10,1... | collective-permute-start | bytes 18440 | tf_op jit(solution)/shard_map/ppermute | solution.py:20
  17.2 27.2 %collective-permute-start.1 = (f32[1,2,6,8,8,2]{5,4,3,2,1,0:T(8,128)S(1)}, f32[1,2,6,8,8,2]{5,4,3,2,1,0:T(8,128)S(1)}, u32[]{:S(2)}, u32[]{:S(2)}) collective-permute-start(f32[1,2,6,8,8,2]{5,4,3,2,1,0:T(8,128)S(1)} %get-tuple-element.70), channel_id=1, source_target_pairs={{1,0},{2,1},{3,2},{4,3},{5,4},{6,5},{7,6},{8,7},{9,8},{10,9},{11,1... | collective-permute-start | bytes 18440 | tf_op jit(solution)/shard_map/ppermute | solution.py:23
  29.1 4.2 %copy-start.5 = (s32[1,2,1]{1,2,0:T(1,128)S(1)}, s32[1,2,1]{1,2,0:T(1,128)}, u32[]{:S(2)}) copy-start(s32[1,2,1]{1,2,0:T(1,128)} %param.7) | copy-start | bytes 28
  45.1 253.6 %copy-start.2 = (f32[6,1,8,128]{3,2,1,0:T(8,128)S(1)}, f32[6,1,8,128]{3,2,1,0:T(8,128)}, u32[]{:S(2)}) copy-start(f32[6,1,8,128]{3,2,1,0:T(8,128)} %slice.758) | copy-start | bytes 73732
  45.1 253.6 %copy-start.3 = (f32[6,1,8,128]{3,2,1,0:T(8,128)S(1)}, f32[6,1,8,128]{3,2,1,0:T(8,128)}, u32[]{:S(2)}) copy-start(f32[6,1,8,128]{3,2,1,0:T(8,128)} %slice.693) | copy-start | bytes 73732
  299.2 64.7 %copy-start.1 = (f32[2,8,8,128]{3,2,1,0:T(8,128)S(1)}, f32[2,8,8,128]{3,2,1,0:T(8,128)}, u32[]{:S(2)}) copy-start(f32[2,8,8,128]{3,2,1,0:T(8,128)} %fusion.111) | copy-start | bytes 196612
Sparse Core Ops, SparseCore 0:
  11.7 142.2 all-gather.7
  157.0 140.7 all-gather.9
  300.0 54.2 all-gather.5
where the time goes:
time: 372 us; the launch traced here: 371 us
  waiting for transfers between devices  306 us (82%)
  between operations  23.6 us (6%)
  starting transfers between devices  16.6 us (4%)
  matrix products  9.63 us (3%)
  local copies, waits for them, and re-layouts  8.67 us (2%)
  other arithmetic  7.18 us (2%)
    all_gather x1, waiting for transfers between devices, per_device(): lax.all_gather(outlet, 'blk', axis=0, tiled=True)  143 us
    all_gather x1, waiting for transfers between devices, per_device(): lax.all_gather(inlet, 'blk', axis=0, tiled=True)  107 us
    all_gather x1, waiting for transfers between devices, per_device(): piece = lax.all_gather(state, 'inst', axis=0, tiled=True)  54.4 us
    ppermute x1, starting transfers between devices, padded_2(): lax.ppermute(lax.slice_in_dim(block, 0, width, axis=dim), axis, backward)  10.9 us
    dot_general x1, matrix products, per_device(): spectral = jnp.tensordot(weights, piece, axes=(0, 0), precision=highest)  9.63 us
  transfers between devices with their start and end apart: 5, of which 3 were waited for; matrix products, arithmetic and copies ran while one was open for 4% of the time, Pallas kernels for 0%

commit v1 on v0

--- a/solution.py
+++ b/solution.py
@@ -130,7 +130,9 @@
     outlet = state[:, 0, :, -2:]
     inlet = state[:, 1, :, 0:2]
     outlet_all, inlet_all = (
-        lax.all_gather(outlet, "blk", axis=0, tiled=True),
+        jnp.concatenate(
+            lax.all_to_all(jnp.stack([outlet] * lax.axis_size("blk")), "blk", 0, 0), axis=0
+        ),
         lax.all_gather(inlet, "blk", axis=0, tiled=True),
     )
     rotor_high = donor_faces(

time: 372 us -> 241 us (0.65)
  waiting for transfers between devices: 306 us -> 163 us
  starting transfers between devices: 16.6 us -> 25.6 us
    all_gather x1 -> x0, waiting for transfers between devices: 143 us -> none  [per_device(): lax.all_gather(outlet, 'blk', axis=0, tiled=True)]
    all_to_all x0 -> x1, starting transfers between devices: none -> 9.08 us  [per_device(): lax.all_to_all(jnp.stack([outlet] * lax.axis_size('blk')), 'blk', 0, 0)]
  transfers between devices with their start and end apart: 5 -> 5, of which waited for: 3 -> 2; matrix products, arithmetic and copies ran while one was open for 4% -> 7% of each run, Pallas kernels for 0% -> 0%
where the time goes in v1:
time: 241 us
  waiting for transfers between devices  163 us (68%)
  starting transfers between devices  25.6 us (11%)
  between operations  23.6 us (10%)
  other arithmetic  10.7 us (4%)
  matrix products  9.63 us (4%)
  local copies, waits for them, and re-layouts  8.15 us (3%)
    all_gather x1, waiting for transfers between devices, per_device(): lax.all_gather(inlet, 'blk', axis=0, tiled=True)  110 us
    all_gather x1, waiting for transfers between devices, per_device(): piece = lax.all_gather(state, 'inst', axis=0, tiled=True)  52 us
    ppermute x1, starting transfers between devices, padded_2(): lax.ppermute(lax.slice_in_dim(block, 0, width, axis=dim), axis, backward)  10.9 us
    dot_general x1, matrix products, per_device(): spectral = jnp.tensordot(weights, piece, axes=(0, 0), precision=highest)  9.63 us
    all_to_all x1, starting transfers between devices, per_device(): lax.all_to_all(jnp.stack([outlet] * lax.axis_size('blk')), 'blk', 0, 0)  9.08 us
    ppermute x1, starting transfers between devices, padded_2(): lax.ppermute(lax.slice_in_dim(block, block.shape[dim] - width, None, axis...  5.64 us
  transfers between devices with their start and end apart: 5, of which 2 were waited for; matrix products, arithmetic and copies ran while one was open for 7% of the time, Pallas kernels for 0%

profile of v1, /device:TPU:1, one launch (start us, length us, event | category | flops | bytes accessed | tf_op | source)
XLA Modules:
  0.0 240.7 jit_solution(2549283254433945969)
XLA Ops:
  7.2 0.0 copy-start.6
  7.2 0.0 copy-start
  7.2 0.0 all-gather.6.cloned.1.call-start
  7.2 1.5 fusion.181
  8.7 0.0 all-gather.6.cloned.1.call-update
  8.8 0.0 all-gather.4.cloned.1.call-start
  8.8 0.7 all-gather.4.cloned.1.call-update
  9.5 1.3 fusion.182
  10.8 5.6 %collective-permute-start = (f32[1,2,6,8,8,2]{5,4,3,2,1,0:T(8,128)S(1)}, f32[1,2,6,8,8,2]{5,4,3,2,1,0:T(8,128)}, u32[]{:S(2)}, u32[]{:S(2)}) collective-permute-start(f32[1,2,6,8,8,2]{5,4,3,2,1,0:T(8,128)S(1)} %get-tuple-element.69), channel_id=1, source_target_pairs={{0,1},{1,2},{2,3},{3,4},{4,5},{5,6},{6,7},{7,8},{8,9},{9,10},{10,1... | collective-permute-start | bytes 18440 | tf_op jit(solution)/shard_map/ppermute | solution.py:20
  16.4 10.9 %collective-permute-start.1 = (f32[1,2,6,8,8,2]{5,4,3,2,1,0:T(8,128)S(1)}, f32[1,2,6,8,8,2]{5,4,3,2,1,0:T(8,128)}, u32[]{:S(2)}, u32[]{:S(2)}) collective-permute-start(f32[1,2,6,8,8,2]{5,4,3,2,1,0:T(8,128)S(1)} %get-tuple-element.70), channel_id=1, source_target_pairs={{1,0},{2,1},{3,2},{4,3},{5,4},{6,5},{7,6},{8,7},{9,8},{10,9},{11,1... | collective-permute-start | bytes 18440 | tf_op jit(solution)/shard_map/ppermute | solution.py:23
  27.3 1.4 stack.24
  28.7 0.0 copy-start.4
  28.7 9.1 %all-to-all-start = ((f32[32,1,6,2,8,128]{5,4,3,2,1,0:T(8,128)}), f32[32,1,6,2,8,128]{5,4,3,2,1,0:T(8,128)S(1)}, u32[]{:S(2)}, u32[]{:S(2)}) async-start(f32[32,1,6,2,8,128]{5,4,3,2,1,0:T(8,128)} %stack.24), calls=%async_computation | async-start | bytes 3145728 | tf_op jit(solution)/shard_map/all_to_all | solution.py:134
  37.8 0.0 copy-done
  37.8 0.0 copy-start.5
  37.9 0.1 rev.13
  38.0 0.1 rev.12
  38.2 0.1 rev.15
  38.3 0.1 rev.14
  38.4 0.0 copy-done.6
  38.4 0.1 broadcast_multiply_fusion.6
  38.5 0.1 pad_maximum_fusion.5
  38.7 0.1 fusion.109
  38.8 0.1 fusion.90
  38.9 0.7 fusion.111
  40.0 0.0 copy-done.4
  40.0 0.6 fusion.185
  40.7 0.4 fusion.26
  41.0 1.1 fusion.12
  42.1 0.0 copy-done.5
  42.1 0.6 fusion.186
  49.1 0.6 slice.696
  49.7 0.6 slice.761
  52.8 0.0 collective-permute-done
  52.9 0.0 collective-permute-done.1
  52.9 1.5 pad_maximum_fusion
  54.4 0.1 fusion.96
  54.5 0.1 fusion.69
  54.6 0.1 add_divide_fusion.2
  54.7 0.1 fusion.64
  54.8 0.1 add_divide_fusion
  55.0 0.1 subtract_maximum_fusion
  55.1 0.1 subtract_maximum_fusion.2
  55.4 0.1 slice_bitcast_fusion.1
  55.5 1.1 fusion.5
  56.5 110.4 %all-gather.6.cloned.1.call-done = f32[32,1,6,2,8,128]{5,4,3,2,1,0:T(8,128)} async-done(((f32[1,1,6,2,8,128]{5,4,3,2,1,0:T(8,128)}), f32[32,1,6,2,8,128]{5,4,3,2,1,0:T(8,128)}) %all-gather.6.cloned.1.call-update) | async-done | bytes 1572880 | tf_op jit(solution)/shard_map/all_gather | solution.py:136
  166.9 0.8 dynamic-slice_bitcast_fusion
  167.7 0.7 fusion.113
  168.4 0.0 all-to-all-done
  168.4 0.0 copy-start.3
  168.4 0.0 copy-start.1
  168.5 0.1 fusion.112
  168.6 0.9 pad_maximum_fusion.11
  169.9 0.0 copy-start.2
  170.0 1.0 fusion.44
  171.0 0.0 copy-done.3
  171.0 0.1 fusion.38
  171.1 0.1 fusion.53
  171.2 0.0 copy-done.1
  171.2 0.1 fusion.50
  171.3 52.0 %all-gather.4.cloned.1.call-done = f32[16,2,6,8,8,128]{5,4,3,2,1,0:T(8,128)} async-done(((f32[1,2,6,8,8,128]{5,4,3,2,1,0:T(8,128)}), f32[16,2,6,8,8,128]{5,4,3,2,1,0:T(8,128)}) %all-gather.4.cloned.1.call-update) | async-done | bytes 6291472 | tf_op jit(solution)/shard_map/all_gather | solution.py:144
  223.3 9.6 %fusion = f32[1,2,6,8,8,128]{5,0,4,3,2,1:T(1,128)S(1)} fusion(f32[16,2,6,8,8,128]{5,4,3,2,1,0:T(8,128)} %all-gather.4.cloned.1.call-done, s32[]{:T(128)S(6)} %axis_index.15), kind=kOutput, calls=%fused_computation | convolution fusion | flops 18874928 | bytes 6684676 | tf_op jit(solution)/shard_map/dot_general | solution.py:147
  232.9 0.0 copy-done.2
  232.9 1.0 subtract_bitcast_fusion
  (56 shorter events, 1.0 us)
Async XLA Ops:
  7.2 31.2 %copy-start.6 = (f32[6]{0:T(128)S(1)}, f32[6]{0:T(128)}, u32[]{:S(2)}) copy-start(f32[6]{0:T(128)} %constant.131.clone) | copy-start | bytes 76
  7.2 30.6 %copy-start = (f32[1,2,6,8,8,128]{5,4,3,2,1,0:T(8,128)S(1)}, f32[1,2,6,8,8,128]{5,4,3,2,1,0:T(8,128)}, u32[]{:S(2)}) copy-start(f32[1,2,6,8,8,128]{5,4,3,2,1,0:T(8,128)} %param.5) | copy-start | bytes 1179652
  7.2 159.7 %all-gather.6.cloned.1.call-start = ((), (), s32[]{:S(2)}) async-start(), calls=%async_computation.2 | async-start | bytes 1622016 | tf_op jit(solution)/shard_map/all_gather | solution.py:136
  8.8 214.5 %all-gather.4.cloned.1.call-start = ((), (), s32[]{:S(2)}) async-start(), calls=%async_computation.1 | async-start | bytes 6684672 | tf_op jit(solution)/shard_map/all_gather | solution.py:144
  10.8 42.1 %collective-permute-start = (f32[1,2,6,8,8,2]{5,4,3,2,1,0:T(8,128)S(1)}, f32[1,2,6,8,8,2]{5,4,3,2,1,0:T(8,128)}, u32[]{:S(2)}, u32[]{:S(2)}) collective-permute-start(f32[1,2,6,8,8,2]{5,4,3,2,1,0:T(8,128)S(1)} %get-tuple-element.69), channel_id=1, source_target_pairs={{0,1},{1,2},{2,3},{3,4},{4,5},{5,6},{6,7},{7,8},{8,9},{9,10},{10,1... | collective-permute-start | bytes 18440 | tf_op jit(solution)/shard_map/ppermute | solution.py:20
  16.4 36.4 %collective-permute-start.1 = (f32[1,2,6,8,8,2]{5,4,3,2,1,0:T(8,128)S(1)}, f32[1,2,6,8,8,2]{5,4,3,2,1,0:T(8,128)}, u32[]{:S(2)}, u32[]{:S(2)}) collective-permute-start(f32[1,2,6,8,8,2]{5,4,3,2,1,0:T(8,128)S(1)} %get-tuple-element.70), channel_id=1, source_target_pairs={{1,0},{2,1},{3,2},{4,3},{5,4},{6,5},{7,6},{8,7},{9,8},{10,9},{11,1... | collective-permute-start | bytes 18440 | tf_op jit(solution)/shard_map/ppermute | solution.py:23
  28.7 11.3 %copy-start.4 = (s32[1,2,1]{1,2,0:T(1,128)S(1)}, s32[1,2,1]{1,2,0:T(1,128)}, u32[]{:S(2)}) copy-start(s32[1,2,1]{1,2,0:T(1,128)} %param.6) | copy-start | bytes 28
  28.7 139.7 %all-to-all-start = ((f32[32,1,6,2,8,128]{5,4,3,2,1,0:T(8,128)}), f32[32,1,6,2,8,128]{5,4,3,2,1,0:T(8,128)S(1)}, u32[]{:S(2)}, u32[]{:S(2)}) async-start(f32[32,1,6,2,8,128]{5,4,3,2,1,0:T(8,128)} %stack.24), calls=%async_computation | async-start | bytes 3145728 | tf_op jit(solution)/shard_map/all_to_all | solution.py:134
  37.8 4.3 %copy-start.5 = (s32[1,2,1]{1,2,0:T(1,128)S(1)}, s32[1,2,1]{1,2,0:T(1,128)}, u32[]{:S(2)}) copy-start(s32[1,2,1]{1,2,0:T(1,128)} %param.7) | copy-start | bytes 28
  168.4 2.5 %copy-start.3 = (f32[6,1,8,128]{3,2,1,0:T(8,128)S(1)}, f32[6,1,8,128]{3,2,1,0:T(8,128)}, u32[]{:S(2)}) copy-start(f32[6,1,8,128]{3,2,1,0:T(8,128)} %slice.761) | copy-start | bytes 73732
  168.4 2.8 %copy-start.1 = (f32[6,8,9,128]{3,2,1,0:T(8,128)S(1)}, f32[6,8,9,128]{3,2,1,0:T(8,128)}, u32[]{:S(2)}) copy-start(f32[6,8,9,128]{3,2,1,0:T(8,128)} %fusion.12) | copy-start | bytes 663556
  169.9 63.1 %copy-start.2 = (f32[2,8,8,128]{3,2,1,0:T(8,128)S(1)}, f32[2,8,8,128]{3,2,1,0:T(8,128)}, u32[]{:S(2)}) copy-start(f32[2,8,8,128]{3,2,1,0:T(8,128)} %fusion.111) | copy-start | bytes 196612
Sparse Core Ops, SparseCore 0:
  11.1 155.7 all-gather.5
  169.0 54.2 all-gather.3
